TPU v7x, 256 devices: a whole 4x4x8 slice. The times are simulated.
256 devices in a mesh: section: 4 (over x_lo, core), dp: 8 (over y, x_hi), expert: 8 (over z).
Axes of the slice: x: 4 (x_hi: 2, x_lo: 2; x = x_hi * 2 + x_lo), y: 4, z: 8, core: 2. Of those that a mesh axis runs over, the one named last changes fastest.
Arguments:
- incoming: bfloat16 [4, 2, 1024, 3584], P('section', None, ('dp', 'expert')), may hold values from -6 to 6
- stash: bfloat16 [4, 2, 1024, 3584], P('section', None, ('dp', 'expert')), may hold values from -6 to 6
- expert_ids: int32 [4, 2, 1024, 2], P('section', None, ('dp', 'expert')), may hold values from 0 to 7, all different within a row; in each aligned block of 16 rows (0 to 15, 16 to 31, ..., all dimensions but the last counted through in order) at most 6 rows name the same one
- route_weight: float32 [4, 2, 1024, 2], P('section', None, ('dp', 'expert')), may hold values from 0.1 to 1
- w_gate: bfloat16 [4, 8, 3584, 2048], P('section', 'expert', None, 'dp'), may hold values from -0.09375 to 0.09375
- w_up: bfloat16 [4, 8, 3584, 2048], P('section', 'expert', None, 'dp'), may hold values from -0.09375 to 0.09375
- w_down: bfloat16 [4, 8, 2048, 3584], P('section', 'expert', 'dp'), may hold values from -0.125 to 0.125
Outputs:
- input_grad: bfloat16 [4, 2, 1024, 3584], P('section', None, ('dp', 'expert'))
- grad_gate: bfloat16 [4, 8, 3584, 2048], P('section', 'expert', None, 'dp')
- grad_up: bfloat16 [4, 8, 3584, 2048], P('section', 'expert', None, 'dp')
- grad_down: bfloat16 [4, 8, 2048, 3584], P('section', 'expert', 'dp')
Inputs may be any that keep to these rules, and one draw needn't show every extreme that they name: `expert_ids`: each token names 2 different experts. Among the 16 tokens of one device in one micro-batch (aligned blocks of rows), no expert is named by more than 6 of them, a bound that some block reaches.
All inputs are finite; a program needn't handle non-finite values.
Results may differ from a plain program's by a relative error of at most 0.01.
Values may be sent and summed in bfloat16 or wider, within the bound.
No kernel may reach another device: no remote copies, remote signals or barrier semaphores. Data moves between devices by JAX's collectives and lax.ppermute only.
A program may use at most 128 MiB of HBM per device.

v0:
```python
import jax
import jax.numpy as jnp
from jax import lax
from jax.sharding import PartitionSpec as P


def passed_along(x, axis, by):
    length = lax.axis_size(axis)
    return lax.ppermute(x, axis, [(i, (i + by) % length) for i in range(length)])


def slice_backward(pair_inputs, pair_scaled, gate_slice, up_slice, down_slice):
    contract_rows = (((0,), (0,)), ((), ()))
    contract_last = (((1,), (1,)), ((), ()))
    gate_pre = jnp.dot(pair_inputs, gate_slice, preferred_element_type=jnp.float32)
    up_pre = jnp.dot(pair_inputs, up_slice, preferred_element_type=jnp.float32)
    logistic = jax.nn.sigmoid(gate_pre)
    activated = gate_pre * logistic
    hidden = (activated * up_pre).astype(jnp.bfloat16)
    hidden_grad = lax.dot_general(
        pair_scaled, down_slice, contract_last, preferred_element_type=jnp.float32
    )
    gate_grad = (hidden_grad * up_pre * logistic * (1.0 + gate_pre * (1.0 - logistic))).astype(
        jnp.bfloat16
    )
    up_grad = (hidden_grad * activated).astype(jnp.bfloat16)
    down_total = lax.dot_general(
        hidden, pair_scaled, contract_rows, preferred_element_type=jnp.float32
    )
    gate_total = lax.dot_general(
        pair_inputs, gate_grad, contract_rows, preferred_element_type=jnp.float32
    )
    up_total = lax.dot_general(
        pair_inputs, up_grad, contract_rows, preferred_element_type=jnp.float32
    )
    partial_back = lax.dot_general(
        gate_grad, gate_slice, contract_last, preferred_element_type=jnp.float32
    )
    partial_back = partial_back + lax.dot_general(
        up_grad, up_slice, contract_last, preferred_element_type=jnp.float32
    )
    return (partial_back, gate_total, up_total, down_total)


def per_device(incoming, stash, expert_ids, route_weight, w_gate, w_up, w_down):
    arrived = passed_along(incoming, "section", -1)
    upstream = arrived[0]
    tokens = stash[0]
    mbatch, tok_rows, model_width = tokens.shape
    top_count = expert_ids.shape[-1]
    experts = lax.axis_size("expert")
    capacity = max(2, 3 * tok_rows * top_count // (2 * experts))
    pair_count = tok_rows * top_count
    slot_count = experts * capacity
    chosen = expert_ids[0].reshape(mbatch, pair_count)
    onehot = (chosen[:, :, None] == jnp.arange(experts, dtype=jnp.int32)[None, None, :]).astype(
        jnp.int32
    )
    running = jnp.cumsum(onehot, axis=1) - 1
    position = jnp.sum(onehot * running, axis=2)
    slot_index = chosen * capacity + position
    pair_slot = slot_index[:, :, None] == jnp.arange(slot_count, dtype=jnp.int32)[None, None, :]
    token_slot = pair_slot.reshape(mbatch, tok_rows, top_count, slot_count).any(axis=2)
    token_slot = token_slot.astype(jnp.bfloat16)
    weight_pairs = route_weight[0].reshape(mbatch, pair_count)
    slot_weight = jnp.sum(jnp.where(pair_slot, weight_pairs[:, :, None], 0.0), axis=1)

    def to_slots(rows):
        gathered = jnp.einsum("mts,mtd->msd", token_slot, rows, preferred_element_type=jnp.float32)
        return gathered

    def by_expert(slots):
        return (
            slots.reshape(mbatch, experts, capacity, model_width)
            .transpose(1, 0, 2, 3)
            .reshape(experts, mbatch * capacity, model_width)
        )

    input_slots = by_expert(to_slots(tokens).astype(jnp.bfloat16))
    sent_inputs = lax.all_to_all(input_slots, "expert", 0, 0, tiled=True)
    recv_inputs = lax.all_gather(sent_inputs, "dp", axis=0, tiled=True)
    scaled_slots = by_expert((slot_weight[:, :, None] * to_slots(upstream)).astype(jnp.bfloat16))
    sent_scaled = lax.all_to_all(scaled_slots, "expert", 0, 0, tiled=True)
    recv_scaled = lax.all_gather(sent_scaled, "dp", axis=0, tiled=True)
    input_rows = recv_inputs.reshape(-1, model_width)
    scaled_rows = recv_scaled.reshape(-1, model_width)
    gate_slice = w_gate[0, 0]
    up_slice = w_up[0, 0]
    down_slice = w_down[0, 0]
    partial_rows, gate_total, up_total, down_total = slice_backward(
        input_rows, scaled_rows, gate_slice, up_slice, down_slice
    )
    sent_back = partial_rows.astype(jnp.bfloat16).reshape(recv_inputs.shape)
    summed = lax.psum_scatter(sent_back, "dp", scatter_dimension=0, tiled=True)
    returned = lax.all_to_all(summed, "expert", 0, 0, tiled=True)
    back_slots = (
        returned.reshape(experts, mbatch, capacity, model_width)
        .transpose(1, 0, 2, 3)
        .reshape(mbatch, slot_count, model_width)
    )
    pair_sum = jnp.einsum(
        "mts,msd->mtd", token_slot, back_slots, preferred_element_type=jnp.float32
    )
    input_grad = (upstream.astype(jnp.float32) + pair_sum).astype(jnp.bfloat16)
    grad_gate = gate_total.astype(jnp.bfloat16)[None, None]
    grad_up = up_total.astype(jnp.bfloat16)[None, None]
    grad_down = down_total.astype(jnp.bfloat16)[None, None]
    return (input_grad[None], grad_gate, grad_up, grad_down)


def solution(mesh):
    return jax.shard_map(
        per_device,
        mesh=mesh,
        in_specs=(
            P("section", None, ("dp", "expert"), None),
            P("section", None, ("dp", "expert"), None),
            P("section", None, ("dp", "expert"), None),
            P("section", None, ("dp", "expert"), None),
            P("section", "expert", None, "dp"),
            P("section", "expert", None, "dp"),
            P("section", "expert", "dp", None),
        ),
        out_specs=(
            P("section", None, ("dp", "expert"), None),
            P("section", "expert", None, "dp"),
            P("section", "expert", None, "dp"),
            P("section", "expert", "dp", None),
        ),
        check_vma=False,
    )
```

profile of v0, /device:TPU:1, one launch (start us, length us, event | category | flops | bytes accessed | tf_op | source)
XLA Modules:
  0.0 409.8 jit_solution(17382456177079624147)
XLA Ops:
  7.2 0.0 copy-start
  7.2 0.0 copy-start.8
  7.2 0.0 copy-start.7
  7.2 0.0 all-gather.5.cloned.1.call-start
  7.2 0.9 copy.59
  8.1 0.1 eq.35
  8.2 0.1 fusion.20
  8.3 0.1 reduce_window_sum.11
  8.4 0.2 select_reduce_fusion.1
  8.6 0.1 reduce_sum.21
  8.6 0.1 copy.60
  8.7 0.7 bitcast_add_fusion
  9.4 0.1 fusion.21
  9.5 1.3 convolution_convert_fusion.3
  10.8 0.7 copy.67
  11.6 0.1 copy.68
  11.7 0.2 copy.69
  11.9 33.6 %all_to_all.15 = bf16[8,12,3584]{2,1,0:T(8,128)(2,1)S(1)} all-to-all(bf16[8,12,3584]{2,1,0:T(8,128)(2,1)S(1)} %copy.69), channel_id=1, replica_groups=mesh['section'=4,'dp'=8,'expert'=8] {'expert'}, dimensions={0} | all-to-all | bytes 1376256 | tf_op jit(solution)/shard_map/all_to_all | solution.py:80
  45.5 1.2 copy.70
  46.8 0.0 all-gather.5.cloned.1.call-update
  46.8 0.0 all-gather.3.cloned.1.call-start
  46.8 2.1 collective-permute-start
  49.0 0.1 copy.61
  49.1 0.1 broadcast_in_dim.30
  49.2 0.1 select_reduce_fusion
  49.3 4.5 %collective-permute-done = bf16[1,2,16,3584]{3,2,1,0:T(8,128)(2,1)S(1)} collective-permute-done((bf16[1,2,16,3584]{3,2,1,0:T(8,128)(2,1)S(1)}, bf16[1,2,16,3584]{3,2,1,0:T(8,128)(2,1)S(1)}, u32[]{:S(2)}, u32[]{:S(2)}) %collective-permute-start) | collective-permute-done | bytes 229408 | tf_op jit(solution)/shard_map/ppermute | solution.py:9
  53.8 0.4 fusion.3
  54.2 0.7 copy.62
  54.9 0.1 copy.63
  55.0 0.2 copy.64
  55.2 27.8 %all_to_all.16 = bf16[8,12,3584]{2,1,0:T(8,128)(2,1)S(1)} all-to-all(bf16[8,12,3584]{2,1,0:T(8,128)(2,1)S(1)} %copy.64), channel_id=1, replica_groups=mesh['section'=4,'dp'=8,'expert'=8] {'expert'}, dimensions={0} | all-to-all | bytes 1376256 | tf_op jit(solution)/shard_map/all_to_all | solution.py:83
  83.0 1.2 copy.65
  84.2 0.0 all-gather.3.cloned.1.call-update
  84.2 0.0 reduce-scatter.2.cloned.1.call-start
  84.3 46.7 %all-gather.5.cloned.1.call-done = bf16[64,12,3584]{2,0,1:T(8,128)(2,1)} async-done(((bf16[8,12,3584]{2,0,1:T(8,128)(2,1)}), bf16[64,12,3584]{2,0,1:T(8,128)(2,1)}) %all-gather.5.cloned.1.call-update) | async-done | bytes 5505040 | tf_op jit(solution)/shard_map/all_gather | solution.py:81
  131.0 8.6 %copy.71 = bf16[64,12,3584]{2,1,0:T(8,128)(2,1)} copy(bf16[64,12,3584]{2,0,1:T(8,128)(2,1)} %all-gather.5.cloned.1.call-done) | data formatting | bytes 11010048 | tf_op jit(solution)/shard_map/all_gather | solution.py:81
  139.6 9.4 %reshape.58 = bf16[768,3584]{1,0:T(8,128)(2,1)} reshape(bf16[64,12,3584]{2,1,0:T(8,128)(2,1)} %copy.71) | data formatting | bytes 11010048 | tf_op jit(solution)/shard_map/reshape | solution.py:85
  149.1 4.3 %fusion.6 = f32[768,256]{1,0:T(8,128)S(1)} fusion(bf16[768,3584]{1,0:T(8,128)(2,1)} %reshape.58, bf16[1,1,3584,256]{3,2,1,0:T(8,128)(2,1)S(1)} %copy-done), kind=kOutput, calls=%fused_computation.12 | convolution fusion | flops 1409286144 | bytes 8126464 | tf_op jit(solution)/shard_map/dot_general | solution.py:15
  153.4 0.5 copy-done.2
  153.8 2.5 fusion.9
  156.3 62.9 %all-gather.3.cloned.1.call-done = bf16[64,12,3584]{2,0,1:T(8,128)(2,1)} async-done(((bf16[8,12,3584]{2,0,1:T(8,128)(2,1)}), bf16[64,12,3584]{2,0,1:T(8,128)(2,1)}) %all-gather.3.cloned.1.call-update) | async-done | bytes 5505040 | tf_op jit(solution)/shard_map/all_gather | solution.py:84
  219.2 8.6 %copy.66 = bf16[64,12,3584]{2,1,0:T(8,128)(2,1)} copy(bf16[64,12,3584]{2,0,1:T(8,128)(2,1)} %all-gather.3.cloned.1.call-done) | data formatting | bytes 11010048 | tf_op jit(solution)/shard_map/all_gather | solution.py:84
  227.8 9.3 %reshape.55 = bf16[768,3584]{1,0:T(8,128)(2,1)} reshape(bf16[64,12,3584]{2,1,0:T(8,128)(2,1)} %copy.66) | data formatting | bytes 11010048 | tf_op jit(solution)/shard_map/reshape | solution.py:86
  237.2 5.0 %multiply_convert_fusion.1 = (bf16[768,256]{1,0:T(8,128)(2,1)S(1)}, bf16[768,256]{1,0:T(8,128)(2,1)S(1)}) fusion(f32[768,256]{1,0:T(8,128)S(1)} %fusion.6, f32[768,256]{1,0:T(8,128)} %fusion.9, bf16[768,3584]{1,0:T(8,128)(2,1)} %reshape.55, bf16[1,1,256,3584]{3,2,1,0:T(8,128)(2,1)} %param.13), kind=kOutput, calls=%fused_computation.20 | convolution fusion | flops 1411842048 | bytes 9699328 | tf_op jit(solution)/shard_map/dot_general | solution.py:20
  242.1 0.0 copy-start.4
  242.2 0.0 copy-start.3
  242.2 1.6 fusion.4
  243.8 0.1 copy-done.3
  244.0 4.0 add_convert_fusion
  248.0 9.2 %reshape.59 = bf16[64,12,3584]{2,1,0:T(8,128)(2,1)} reshape(bf16[768,3584]{1,0:T(8,128)(2,1)} %add_convert_fusion) | data formatting | bytes 11010048 | tf_op jit(solution)/shard_map/reshape | solution.py:93
  257.2 0.0 reduce-scatter.2.cloned.1.call-update
  257.3 109.4 %reduce-scatter.2.cloned.1.call-done = bf16[8,12,3584]{2,1,0:T(8,128)(2,1)} async-done(((bf16[64,12,3584]{2,1,0:T(8,128)(2,1)}), bf16[8,12,3584]{2,1,0:T(8,128)(2,1)}) %reduce-scatter.2.cloned.1.call-update) | async-done | bytes 688144 | tf_op jit(solution)/shard_map/reduce_scatter | solution.py:94
  366.7 6.9 %all-to-all-start.2 = ((bf16[8,12,3584]{2,1,0:T(8,128)(2,1)}), bf16[8,12,3584]{2,1,0:T(8,128)(2,1)}, u32[]{:S(2)}, u32[]{:S(2)}) async-start(bf16[8,12,3584]{2,1,0:T(8,128)(2,1)} %reduce-scatter.2.cloned.1.call-done), calls=%async_computation.3 | async-start | bytes 1835008 | tf_op jit(solution)/shard_map/all_to_all | solution.py:95
  373.6 0.0 copy-start.5
  373.6 0.0 slice-start.2
  373.6 5.7 %fusion.1 = bf16[1,1,3584,256]{3,2,1,0:T(8,128)(2,1)} fusion(bf16[768,3584]{1,0:T(8,128)(2,1)} %reshape.58, bf16[768,256]{1,0:T(8,128)(2,1)} %copy-done.6), kind=kOutput, calls=%fused_computation.5 | convolution fusion | flops 1410203648 | bytes 7733248 | tf_op jit(solution)/shard_map/dot_general | solution.py:33
  379.2 0.0 slice-start.3
  379.3 0.0 copy-start.11
  379.3 2.9 fusion
  382.2 2.9 fusion.2
  385.1 14.9 %all-to-all-done.2 = bf16[8,12,3584]{2,1,0:T(8,128)(2,1)} async-done(((bf16[8,12,3584]{2,1,0:T(8,128)(2,1)}), bf16[8,12,3584]{2,1,0:T(8,128)(2,1)}, u32[]{:S(2)}, u32[]{:S(2)}) %all-to-all-start.2) | async-done | bytes 688160 | tf_op jit(solution)/shard_map/all_to_all | solution.py:95
  400.0 1.6 copy.72
  401.6 0.7 copy.73
  402.3 0.9 fusion.16
  (24 shorter events, 0.0 us)
Async XLA Ops:
  7.2 141.9 %copy-start = (bf16[1,1,3584,256]{3,2,1,0:T(8,128)(2,1)S(1)}, bf16[1,1,3584,256]{3,2,1,0:T(8,128)(2,1)}, u32[]{:S(2)}) copy-start(bf16[1,1,3584,256]{3,2,1,0:T(8,128)(2,1)} %param.11) | copy-start | bytes 5505028
  7.2 39.7 %copy-start.8 = (bf16[1,2,16,3584]{3,2,1,0:T(8,128)(2,1)S(1)}, bf16[1,2,16,3584]{3,2,1,0:T(8,128)(2,1)}, u32[]{:S(2)}) copy-start(bf16[1,2,16,3584]{3,2,1,0:T(8,128)(2,1)} %param.7) | copy-start | bytes 688132
  7.2 41.8 %copy-start.7 = (f32[1,2,16,2]{2,3,1,0:T(2,128)S(1)}, f32[1,2,16,2]{2,3,1,0:T(2,128)}, u32[]{:S(2)}) copy-start(f32[1,2,16,2]{2,3,1,0:T(2,128)} %param.10) | copy-start | bytes 772
  7.2 123.8 %all-gather.5.cloned.1.call-start = ((), (), s32[]{:S(2)}) async-start(), calls=%async_computation.5 | async-start | bytes 6193152 | tf_op jit(solution)/shard_map/all_gather | solution.py:81
  46.8 172.4 %all-gather.3.cloned.1.call-start = ((), (), s32[]{:S(2)}) async-start(), calls=%async_computation.4 | async-start | bytes 6193152 | tf_op jit(solution)/shard_map/all_gather | solution.py:84
  46.8 6.9 %collective-permute-start = (bf16[1,2,16,3584]{3,2,1,0:T(8,128)(2,1)S(1)}, bf16[1,2,16,3584]{3,2,1,0:T(8,128)(2,1)S(1)}, u32[]{:S(2)}, u32[]{:S(2)}) collective-permute-start(bf16[1,2,16,3584]{3,2,1,0:T(8,128)(2,1)S(1)} %copy-done.8), channel_id=1, source_target_pairs={{0,192},{64,0},{128,64},{192,128},{1,193},{65,1},{129,65},{193,129... | collective-permute-start | bytes 688136 | tf_op jit(solution)/shard_map/ppermute | solution.py:9
  84.2 282.4 %reduce-scatter.2.cloned.1.call-start = ((), (), s32[]{:S(2)}) async-start(), calls=%async_computation.6 | async-start | bytes 8257536 | tf_op jit(solution)/shard_map/reduce_scatter | solution.py:94
  149.1 4.3 %copy-start.1 = (bf16[768,3584]{1,0:T(8,128)(2,1)S(1)}, bf16[768,3584]{1,0:T(8,128)(2,1)}, u32[]{:S(2)}) copy-start(bf16[768,3584]{1,0:T(8,128)(2,1)} %reshape.58) | copy-start | bytes 16515076
  149.1 4.8 %copy-start.2 = (bf16[1,1,3584,256]{3,2,1,0:T(8,128)(2,1)S(1)}, bf16[1,1,3584,256]{3,2,1,0:T(8,128)(2,1)}, u32[]{:S(2)}) copy-start(bf16[1,1,3584,256]{3,2,1,0:T(8,128)(2,1)} %param.12) | copy-start | bytes 5505028
  153.8 83.3 %copy-start.9 = (f32[768,256]{1,0:T(8,128)}, f32[768,256]{1,0:T(8,128)S(1)}, u32[]{:S(2)}) copy-start(f32[768,256]{1,0:T(8,128)S(1)} %fusion.6) | copy-start | bytes 2359300
  242.1 1.7 copy-start.4
  242.2 1.7 copy-start.6
  242.2 1.8 copy-start.3
  366.7 12.6 %slice-start = ((s8[5505024]{0:T(1024)(128)(4,1)}), s8[1310720]{0:T(1024)(128)(4,1)S(1)}, s32[]{:S(2)}) async-start(s8[5505024]{0:T(1024)(128)(4,1)} %bitcast.61), calls=%async_computation.7 | async-start | bytes 2621440
  366.7 33.4 %all-to-all-start.2 = ((bf16[8,12,3584]{2,1,0:T(8,128)(2,1)}), bf16[8,12,3584]{2,1,0:T(8,128)(2,1)}, u32[]{:S(2)}, u32[]{:S(2)}) async-start(bf16[8,12,3584]{2,1,0:T(8,128)(2,1)} %reduce-scatter.2.cloned.1.call-done), calls=%async_computation.3 | async-start | bytes 1835008 | tf_op jit(solution)/shard_map/all_to_all | solution.py:95
  373.5 5.7 %slice-start.1 = ((s8[5505024]{0:T(1024)(128)(4,1)}), s8[4194304]{0:T(1024)(128)(4,1)S(1)}, s32[]{:S(2)}) async-start(s8[5505024]{0:T(1024)(128)(4,1)} %bitcast.61), calls=%async_computation.8 | async-start | bytes 8388608
  373.6 5.7 %copy-start.5 = (bf16[768,256]{1,0:T(8,128)(2,1)S(1)}, bf16[768,256]{1,0:T(8,128)(2,1)}, u32[]{:S(2)}) copy-start(bf16[768,256]{1,0:T(8,128)(2,1)} %copy-done.4) | copy-start | bytes 1179652
  373.6 8.6 %slice-start.2 = ((s8[5505024]{0:T(1024)(128)(4,1)}), s8[4194304]{0:T(1024)(128)(4,1)S(1)}, s32[]{:S(2)}) async-start(s8[5505024]{0:T(1024)(128)(4,1)} %bitcast.63), calls=%async_computation.9 | async-start | bytes 8388608
  379.2 2.9 slice-start.3
  379.3 2.9 copy-start.10
  379.3 2.9 copy-start.11
Sparse Core Ops, SparseCore 0:
  46.9 84.0 all-gather.4
  134.2 84.9 all-gather.2
  257.4 109.2 reduce-scatter.1
where the time goes:
time: 411 us; the launch traced here: 410 us
  waiting for transfers between devices  238 us (58%)
  blocking collectives  61.4 us (15%)
  local copies, waits for them, and re-layouts  54.1 us (13%)
  matrix products  31.5 us (8%)
  between operations  14 us (3%)
  starting transfers between devices  9.14 us (2%)
    reduce_scatter x1, waiting for transfers between devices, per_device(): summed = lax.psum_scatter(sent_back, 'dp', scatter_dimension=0, tiled=True)  109 us
    all_gather x1, waiting for transfers between devices, per_device(): recv_scaled = lax.all_gather(sent_scaled, 'dp', axis=0, tiled=True)  62.9 us
    all_gather x1, waiting for transfers between devices, per_device(): recv_inputs = lax.all_gather(sent_inputs, 'dp', axis=0, tiled=True)  46.7 us
    all_to_all x1, blocking collectives, per_device(): sent_inputs = lax.all_to_all(input_slots, 'expert', 0, 0, tiled=True)  33.6 us
    all_to_all x1, blocking collectives, per_device(): sent_scaled = lax.all_to_all(scaled_slots, 'expert', 0, 0, tiled=True)  27.8 us
    all_to_all x1, waiting for transfers between devices, per_device(): returned = lax.all_to_all(summed, 'expert', 0, 0, tiled=True)  14.9 us
    reshape x1, local copies, waits for them, and re-layouts, per_device(): input_rows = recv_inputs.reshape(-1, model_width)  9.45 us
    reshape x1, local copies, waits for them, and re-layouts, per_device(): scaled_rows = recv_scaled.reshape(-1, model_width)  9.34 us
  transfers between devices with their start and end apart: 5, of which 5 were waited for; matrix products, arithmetic and copies ran while one was open for 10% of the time, Pallas kernels for 0%

commit v1 on v0

--- a/solution.py
+++ b/solution.py
@@ -81,7 +81,9 @@
     recv_inputs = lax.all_gather(sent_inputs, "dp", axis=0, tiled=True)
     scaled_slots = by_expert((slot_weight[:, :, None] * to_slots(upstream)).astype(jnp.bfloat16))
     sent_scaled = lax.all_to_all(scaled_slots, "expert", 0, 0, tiled=True)
-    recv_scaled = lax.all_gather(sent_scaled, "dp", axis=0, tiled=True)
+    recv_scaled = jnp.concatenate(
+        lax.all_to_all(jnp.stack([sent_scaled] * lax.axis_size("dp")), "dp", 0, 0), axis=0
+    )
     input_rows = recv_inputs.reshape(-1, model_width)
     scaled_rows = recv_scaled.reshape(-1, model_width)
     gate_slice = w_gate[0, 0]

time: 411 us -> 389 us (0.946)
  waiting for transfers between devices: 238 us -> 126 us
  blocking collectives: 61.4 us -> 159 us
  local copies, waits for them, and re-layouts: 54.1 us -> 49.6 us
    all_to_all x0 -> x1, blocking collectives: none -> 97.4 us  [per_device(): lax.all_to_all(jnp.stack([sent_scaled] * lax.axis_size('dp')), 'dp', 0, 0)]
    all_gather x1 -> x0, waiting for transfers between devices: 62.9 us -> none  [per_device(): recv_scaled = lax.all_gather(sent_scaled, 'dp', axis=0, tiled=True)]
    all_gather x1, waiting for transfers between devices: 46.7 us -> 0.01 us  [per_device(): recv_inputs = lax.all_gather(sent_inputs, 'dp', axis=0, tiled=True)]
    another operation x0 -> x2, local copies, waits for them, and re-layouts: none -> 9.82 us  [the longest x1 9.36 us: per_device(): scaled_rows = recv_scaled.reshape(-1, model_width)]
    reshape x1 -> x0, local copies, waits for them, and re-layouts: 9.34 us -> none  [per_device(): scaled_rows = recv_scaled.reshape(-1, model_width)]
    all_gather x1 -> x0, local copies, waits for them, and re-layouts: 8.62 us -> none  [per_device(): recv_scaled = lax.all_gather(sent_scaled, 'dp', axis=0, tiled=True)]
    all_to_all x0 -> x1, local copies, waits for them, and re-layouts: none -> 5.03 us  [per_device(): lax.all_to_all(jnp.stack([sent_scaled] * lax.axis_size('dp')), 'dp', 0, 0)]
  transfers between devices with their start and end apart: 5 -> 4, of which waited for: 5 -> 3; matrix products, arithmetic and copies ran while one was open for 10% -> 7% of each run, Pallas kernels for 0% -> 0%
where the time goes in v1:
time: 389 us; the launch traced here: 388 us
  blocking collectives  159 us (41%)
  waiting for transfers between devices  126 us (32%)
  local copies, waits for them, and re-layouts  49.6 us (13%)
  matrix products  29.3 us (8%)
  between operations  14.4 us (4%)
  starting transfers between devices  8.93 us (2%)
    reduce_scatter x1, waiting for transfers between devices, per_device(): summed = lax.psum_scatter(sent_back, 'dp', scatter_dimension=0, tiled=True)  107 us
    all_to_all x1, blocking collectives, per_device(): lax.all_to_all(jnp.stack([sent_scaled] * lax.axis_size('dp')), 'dp', 0, 0)  97.4 us
    all_to_all x1, blocking collectives, per_device(): sent_inputs = lax.all_to_all(input_slots, 'expert', 0, 0, tiled=True)  33.6 us
    all_to_all x1, blocking collectives, per_device(): sent_scaled = lax.all_to_all(scaled_slots, 'expert', 0, 0, tiled=True)  27.8 us
    all_to_all x1, waiting for transfers between devices, per_device(): returned = lax.all_to_all(summed, 'expert', 0, 0, tiled=True)  14.9 us
    another operation x1, local copies, waits for them, and re-layouts, per_device(): scaled_rows = recv_scaled.reshape(-1, model_width)  9.36 us
    reshape x1, local copies, waits for them, and re-layouts, per_device(): input_rows = recv_inputs.reshape(-1, model_width)  9.35 us
    reshape x1, local copies, waits for them, and re-layouts, per_device(): sent_back = partial_rows.astype(jnp.bfloat16).reshape(recv_inputs.shape)  9.26 us
  transfers between devices with their start and end apart: 4, of which 3 were waited for; matrix products, arithmetic and copies ran while one was open for 7% of the time, Pallas kernels for 0%

profile of v1, /device:TPU:1, one launch (start us, length us, event | category | flops | bytes accessed | tf_op | source)
XLA Modules:
  0.0 388.3 jit_solution(7210610336454479202)
XLA Ops:
  7.2 0.0 copy-start
  7.2 0.0 copy-start.8
  7.2 0.0 copy-start.6
  7.2 0.0 all-gather.2.cloned.1.call-start
  7.2 0.9 copy.61
  8.1 0.1 eq.35
  8.2 0.1 fusion.20
  8.3 0.1 reduce_window_sum.11
  8.4 0.2 select_reduce_fusion.1
  8.6 0.1 reduce_sum.21
  8.6 0.1 copy.62
  8.7 0.7 bitcast_add_fusion
  9.4 0.1 fusion.21
  9.5 1.3 convolution_convert_fusion.3
  10.8 0.7 copy.69
  11.6 0.1 copy.70
  11.7 0.2 copy.71
  11.9 33.6 %all_to_all.20 = bf16[8,12,3584]{2,1,0:T(8,128)(2,1)S(1)} all-to-all(bf16[8,12,3584]{2,1,0:T(8,128)(2,1)S(1)} %copy.71), channel_id=1, replica_groups=mesh['section'=4,'dp'=8,'expert'=8] {'expert'}, dimensions={0} | all-to-all | bytes 1376256 | tf_op jit(solution)/shard_map/all_to_all | solution.py:80
  45.5 1.2 copy.72
  46.8 0.0 all-gather.2.cloned.1.call-update
  46.8 0.0 reduce-scatter.2.cloned.1.call-start
  46.8 2.1 collective-permute-start
  49.0 0.1 copy.63
  49.1 0.1 broadcast_in_dim.30
  49.2 0.1 select_reduce_fusion
  49.3 4.5 %collective-permute-done = bf16[1,2,16,3584]{3,2,1,0:T(8,128)(2,1)S(1)} collective-permute-done((bf16[1,2,16,3584]{3,2,1,0:T(8,128)(2,1)S(1)}, bf16[1,2,16,3584]{3,2,1,0:T(8,128)(2,1)S(1)}, u32[]{:S(2)}, u32[]{:S(2)}) %collective-permute-start) | collective-permute-done | bytes 229408 | tf_op jit(solution)/shard_map/ppermute | solution.py:9
  53.8 0.4 fusion.3
  54.2 0.7 copy.64
  54.9 0.1 copy.65
  55.0 0.2 copy.66
  55.2 27.8 %all_to_all.21 = bf16[8,12,3584]{2,1,0:T(8,128)(2,1)S(1)} all-to-all(bf16[8,12,3584]{2,1,0:T(8,128)(2,1)S(1)} %copy.66), channel_id=1, replica_groups=mesh['section'=4,'dp'=8,'expert'=8] {'expert'}, dimensions={0} | all-to-all | bytes 1376256 | tf_op jit(solution)/shard_map/all_to_all | solution.py:83
  83.0 0.4 copy.67
  83.4 0.5 stack.2
  83.8 97.4 %all_to_all.22 = bf16[8,8,12,3584]{3,1,2,0:T(8,128)(2,1)S(1)} all-to-all(bf16[8,8,12,3584]{3,1,2,0:T(8,128)(2,1)S(1)} %stack.2), channel_id=1, replica_groups=mesh['section'=4,'dp'=8,'expert'=8] {'dp'}, dimensions={0} | all-to-all | bytes 11010048 | tf_op jit(solution)/shard_map/all_to_all | solution.py:85
  181.3 5.0 %copy.68 = bf16[8,8,12,3584]{3,2,1,0:T(8,128)(2,1)} copy(bf16[8,8,12,3584]{3,1,2,0:T(8,128)(2,1)S(1)} %all_to_all.22) | data formatting | bytes 11010048 | tf_op jit(solution)/shard_map/all_to_all | solution.py:85
  186.3 9.4 %reshape_reshape.3 = bf16[768,3584]{1,0:T(8,128)(2,1)} reshape(bf16[8,8,12,3584]{3,2,1,0:T(8,128)(2,1)} %copy.68) | data formatting | bytes 11010048 | tf_op jit(solution)/shard_map/reshape;reshape | solution.py:88
  195.7 8.6 %copy.73 = bf16[64,12,3584]{2,1,0:T(8,128)(2,1)} copy(bf16[64,12,3584]{2,0,1:T(8,128)(2,1)} %all-gather.2.cloned.1.call-done) | data formatting | bytes 11010048 | tf_op jit(solution)/shard_map/all_gather | solution.py:81
  204.3 9.4 %reshape.56 = bf16[768,3584]{1,0:T(8,128)(2,1)} reshape(bf16[64,12,3584]{2,1,0:T(8,128)(2,1)} %copy.73) | data formatting | bytes 11010048 | tf_op jit(solution)/shard_map/reshape | solution.py:87
  213.7 4.3 %fusion.6 = f32[768,256]{1,0:T(8,128)S(1)} fusion(bf16[768,3584]{1,0:T(8,128)(2,1)} %reshape.56, bf16[1,1,3584,256]{3,2,1,0:T(8,128)(2,1)S(1)} %copy-done), kind=kOutput, calls=%fused_computation.12 | convolution fusion | flops 1409286144 | bytes 8126464 | tf_op jit(solution)/shard_map/dot_general | solution.py:15
  218.0 0.0 slice-start.1
  218.0 0.0 copy-start.7
  218.0 3.5 fusion.9
  221.5 0.0 copy-start.11
  221.6 1.8 multiply_convert_fusion.1
  223.3 0.0 copy-start.3
  223.4 0.0 copy-start.2
  223.4 1.6 fusion.4
  225.0 0.1 copy-done.2
  225.2 4.0 %add_convert_fusion = bf16[768,3584]{1,0:T(8,128)(2,1)} fusion(f32[768,3584]{1,0:T(8,128)S(1)} %fusion.4, bf16[768,256]{1,0:T(8,128)(2,1)S(1)} %get-tuple-element.4, bf16[1,1,3584,256]{3,2,1,0:T(8,128)(2,1)S(1)} %copy-done.2), kind=kOutput, calls=%fused_computation | convolution fusion | flops 1414791168 | bytes 18743296 | tf_op jit(solution)/shard_map/dot_general | solution.py:39
  229.2 9.3 %reshape.57 = bf16[64,12,3584]{2,1,0:T(8,128)(2,1)} reshape(bf16[768,3584]{1,0:T(8,128)(2,1)} %add_convert_fusion) | data formatting | bytes 11010048 | tf_op jit(solution)/shard_map/reshape | solution.py:95
  238.4 0.0 reduce-scatter.2.cloned.1.call-update
  238.5 106.6 %reduce-scatter.2.cloned.1.call-done = bf16[8,12,3584]{2,1,0:T(8,128)(2,1)} async-done(((bf16[64,12,3584]{2,1,0:T(8,128)(2,1)}), bf16[8,12,3584]{2,1,0:T(8,128)(2,1)}) %reduce-scatter.2.cloned.1.call-update) | async-done | bytes 688144 | tf_op jit(solution)/shard_map/reduce_scatter | solution.py:96
  345.0 6.7 %all-to-all-start.3 = ((bf16[8,12,3584]{2,1,0:T(8,128)(2,1)}), bf16[8,12,3584]{2,1,0:T(8,128)(2,1)}, u32[]{:S(2)}, u32[]{:S(2)}) async-start(bf16[8,12,3584]{2,1,0:T(8,128)(2,1)} %reduce-scatter.2.cloned.1.call-done), calls=%async_computation.4 | async-start | bytes 1835008 | tf_op jit(solution)/shard_map/all_to_all | solution.py:97
  351.8 0.0 copy-start.4
  351.8 0.0 slice-start.2
  351.8 5.6 %fusion.1 = bf16[1,1,3584,256]{3,2,1,0:T(8,128)(2,1)} fusion(bf16[768,3584]{1,0:T(8,128)(2,1)} %reshape.56, bf16[768,256]{1,0:T(8,128)(2,1)} %copy-done.5), kind=kOutput, calls=%fused_computation.5 | convolution fusion | flops 1410203648 | bytes 7733248 | tf_op jit(solution)/shard_map/dot_general | solution.py:33
  357.5 0.0 slice-start.3
  357.5 0.0 copy-start.12
  357.5 2.9 fusion
  360.4 2.9 fusion.2
  363.3 14.9 %all-to-all-done.3 = bf16[8,12,3584]{2,1,0:T(8,128)(2,1)} async-done(((bf16[8,12,3584]{2,1,0:T(8,128)(2,1)}), bf16[8,12,3584]{2,1,0:T(8,128)(2,1)}, u32[]{:S(2)}, u32[]{:S(2)}) %all-to-all-start.3) | async-done | bytes 688160 | tf_op jit(solution)/shard_map/all_to_all | solution.py:97
  378.3 1.6 copy.74
  379.8 0.7 copy.75
  380.5 0.9 fusion.16
  (30 shorter events, 0.1 us)
Async XLA Ops:
  7.2 206.5 %copy-start = (bf16[1,1,3584,256]{3,2,1,0:T(8,128)(2,1)S(1)}, bf16[1,1,3584,256]{3,2,1,0:T(8,128)(2,1)}, u32[]{:S(2)}) copy-start(bf16[1,1,3584,256]{3,2,1,0:T(8,128)(2,1)} %param.11) | copy-start | bytes 5505028
  7.2 39.7 %copy-start.8 = (bf16[1,2,16,3584]{3,2,1,0:T(8,128)(2,1)S(1)}, bf16[1,2,16,3584]{3,2,1,0:T(8,128)(2,1)}, u32[]{:S(2)}) copy-start(bf16[1,2,16,3584]{3,2,1,0:T(8,128)(2,1)} %param.7) | copy-start | bytes 688132
  7.2 41.8 %copy-start.6 = (f32[1,2,16,2]{2,3,1,0:T(2,128)S(1)}, f32[1,2,16,2]{2,3,1,0:T(2,128)}, u32[]{:S(2)}) copy-start(f32[1,2,16,2]{2,3,1,0:T(2,128)} %param.10) | copy-start | bytes 772
  7.2 188.5 %all-gather.2.cloned.1.call-start = ((), (), s32[]{:S(2)}) async-start(), calls=%async_computation.5 | async-start | bytes 6193152 | tf_op jit(solution)/shard_map/all_gather | solution.py:81
  46.8 298.3 %reduce-scatter.2.cloned.1.call-start = ((), (), s32[]{:S(2)}) async-start(), calls=%async_computation.6 | async-start | bytes 8257536 | tf_op jit(solution)/shard_map/reduce_scatter | solution.py:96
  46.8 6.9 %collective-permute-start = (bf16[1,2,16,3584]{3,2,1,0:T(8,128)(2,1)S(1)}, bf16[1,2,16,3584]{3,2,1,0:T(8,128)(2,1)S(1)}, u32[]{:S(2)}, u32[]{:S(2)}) collective-permute-start(bf16[1,2,16,3584]{3,2,1,0:T(8,128)(2,1)S(1)} %copy-done.8), channel_id=1, source_target_pairs={{0,192},{64,0},{128,64},{192,128},{1,193},{65,1},{129,65},{193,129... | collective-permute-start | bytes 688136 | tf_op jit(solution)/shard_map/ppermute | solution.py:9
  213.7 4.3 %copy-start.1 = (bf16[768,3584]{1,0:T(8,128)(2,1)S(1)}, bf16[768,3584]{1,0:T(8,128)(2,1)}, u32[]{:S(2)}) copy-start(bf16[768,3584]{1,0:T(8,128)(2,1)} %reshape.56) | copy-start | bytes 16515076
  213.7 7.8 %slice-start = ((s8[5505024]{0:T(1024)(128)(4,1)}), s8[4194304]{0:T(1024)(128)(4,1)S(1)}, s32[]{:S(2)}) async-start(s8[5505024]{0:T(1024)(128)(4,1)} %bitcast.61), calls=%async_computation.7 | async-start | bytes 8388608
  218.0 5.3 %copy-start.9 = (f32[768,256]{1,0:T(8,128)}, f32[768,256]{1,0:T(8,128)S(1)}, u32[]{:S(2)}) copy-start(f32[768,256]{1,0:T(8,128)S(1)} %fusion.6) | copy-start | bytes 2359300
  218.0 3.5 slice-start.1
  218.0 3.5 copy-start.7
  221.5 1.8 copy-start.11
  223.3 1.7 copy-start.3
  223.4 1.7 copy-start.5
  223.4 1.8 copy-start.2
  238.4 119.0 %slice-start.4 = ((s8[5505024]{0:T(1024)(128)(4,1)}), s8[1310720]{0:T(1024)(128)(4,1)S(1)}, s32[]{:S(2)}) async-start(s8[5505024]{0:T(1024)(128)(4,1)} %bitcast.65), calls=%async_computation.11 | async-start | bytes 2621440
  345.0 33.2 %all-to-all-start.3 = ((bf16[8,12,3584]{2,1,0:T(8,128)(2,1)}), bf16[8,12,3584]{2,1,0:T(8,128)(2,1)}, u32[]{:S(2)}, u32[]{:S(2)}) async-start(bf16[8,12,3584]{2,1,0:T(8,128)(2,1)} %reduce-scatter.2.cloned.1.call-done), calls=%async_computation.4 | async-start | bytes 1835008 | tf_op jit(solution)/shard_map/all_to_all | solution.py:97
  351.8 5.7 %slice-start.5 = ((s8[5505024]{0:T(1024)(128)(4,1)}), s8[4194304]{0:T(1024)(128)(4,1)S(1)}, s32[]{:S(2)}) async-start(s8[5505024]{0:T(1024)(128)(4,1)} %bitcast.65), calls=%async_computation.12 | async-start | bytes 8388608
  351.8 5.7 %copy-start.4 = (bf16[768,256]{1,0:T(8,128)(2,1)S(1)}, bf16[768,256]{1,0:T(8,128)(2,1)}, u32[]{:S(2)}) copy-start(bf16[768,256]{1,0:T(8,128)(2,1)} %copy-done.3) | copy-start | bytes 1179652
  351.8 8.6 %slice-start.2 = ((s8[5505024]{0:T(1024)(128)(4,1)}), s8[4194304]{0:T(1024)(128)(4,1)S(1)}, s32[]{:S(2)}) async-start(s8[5505024]{0:T(1024)(128)(4,1)} %bitcast.63), calls=%async_computation.9 | async-start | bytes 8388608
  357.5 2.9 slice-start.3
  357.5 2.9 copy-start.10
  357.5 2.9 copy-start.12
Sparse Core Ops, SparseCore 0:
  46.9 115.8 all-gather.1
  238.6 106.4 reduce-scatter.1
